TPU v7x, 128 devices: a whole 4x4x4 slice. The times are simulated.
128 devices in a mesh: gx: 4 (over x_lo, core), gy: 8 (over y, x_hi), gz: 4 (over z).
Axes of the slice: x: 4 (x_hi: 2, x_lo: 2; x = x_hi * 2 + x_lo), y: 4, z: 4, core: 2. Of those that a mesh axis runs over, the one named last changes fastest.
Arguments:
- state: float32 [4, 96, 128, 2048], P(None, 'gz', 'gx', 'gy'), may hold values from -5 to 5
- mixing: float32 [2, 96, 128, 2048], P(None, 'gz', 'gx', 'gy'), may hold values from 0.1 to 1000
- depth_levels: int32 [128, 2048], replicated, may hold values from 0 to 96
- wind: float32 [2, 128, 2048], P(None, 'gx', 'gy'), may hold values from -3 to 3
Outputs:
- state_next: float32 [4, 96, 128, 2048], P(None, 'gz', 'gx', 'gy')
Inputs may be any that keep to these rules, and one draw needn't show every extreme that they name: `depth_levels`: levels at or beyond a column's count are land.
All inputs are finite; a program needn't handle non-finite values.
Results may differ from a plain program's by a relative error of at most 0.0003.
Values sent between devices are 32-bit elements; how exact they have to be, the bound alone decides.
No kernel may reach another device: no remote copies, remote signals or barrier semaphores. Data moves between devices by JAX's collectives and lax.ppermute only.
A program may use at most 192 MiB of HBM per device.

v0:
```python
import jax
import jax.numpy as jnp
from jax import lax
from jax.sharding import PartitionSpec as P


def padded_2(array, sides, width):
    for axis, dim in sides:
        peers, length = (lax.axis_size(axis), array.shape[dim])
        up = [(i, (i + 1) % peers) for i in range(peers)]
        down = [(j, i) for i, j in up]
        last = lax.slice_in_dim(array, length - width, length, axis=dim)
        initial = lax.slice_in_dim(array, 0, width, axis=dim)
        before = lax.ppermute(last, axis, up)
        after = lax.ppermute(initial, axis, down)
        array = jnp.concatenate([before, array, after], axis=dim)
    return array


def carried_in(part, axis, combine, identity):
    place = lax.axis_index(axis)
    gathered = lax.all_gather(part, axis)
    state = jnp.zeros_like(part) + jnp.asarray(identity, part.dtype)

    def one(turn, state):
        return combine(state, lax.dynamic_index_in_dim(gathered, turn, 0, False))

    return lax.fori_loop(0, place, one, state)


def density_of(fields, wet_mask):
    return (-0.3 * fields[0] + 0.7 * fields[1] - 0.05 * fields[0] * fields[0]) * wet_mask


def advance(padded, wet_pad, pressure, wall_face, coriolis):
    wet_x = wet_pad[:, :-1, 1:-1] * wet_pad[:, 1:, 1:-1]
    wet_y = wet_pad[:, 1:-1, :-1] * wet_pad[:, 1:-1, 1:] * wall_face
    east_vel = 0.5 * (padded[2, :, :-1, 1:-1] + padded[2, :, 1:, 1:-1]) * wet_x
    north_vel = 0.5 * (padded[3, :, 1:-1, :-1] + padded[3, :, 1:-1, 1:]) * wet_y
    west_side = padded[:, :, :-1, 1:-1]
    east_side = padded[:, :, 1:, 1:-1]
    flux_x = 0.25 * (
        jnp.maximum(east_vel, 0.0) * west_side + jnp.minimum(east_vel, 0.0) * east_side
    ) - 0.08 * wet_x * (east_side - west_side)
    south_side = padded[:, :, 1:-1, :-1]
    north_side = padded[:, :, 1:-1, 1:]
    flux_y = 0.25 * (
        jnp.maximum(north_vel, 0.0) * south_side + jnp.minimum(north_vel, 0.0) * north_side
    ) - 0.08 * wet_y * (north_side - south_side)
    interior = padded[:, :, 1:-1, 1:-1]
    moved = interior - (
        flux_x[:, :, 1:] - flux_x[:, :, :-1] + flux_y[:, :, :, 1:] - flux_y[:, :, :, :-1]
    )
    centre = pressure[:, 1:-1, 1:-1]
    grad_x = 0.5 * (
        wet_x[:, 1:] * (pressure[:, 2:, 1:-1] - centre)
        + wet_x[:, :-1] * (centre - pressure[:, :-2, 1:-1])
    )
    grad_y = 0.5 * (
        wet_y[:, :, 1:] * (pressure[:, 1:-1, 2:] - centre)
        + wet_y[:, :, :-1] * (centre - pressure[:, 1:-1, :-2])
    )
    east_new = moved[2] + 0.3 * coriolis * interior[3] - grad_x
    north_new = moved[3] - 0.3 * coriolis * interior[2] - grad_y
    wet_inner = wet_pad[:, 1:-1, 1:-1]
    return jnp.stack([moved[0], moved[1], east_new, north_new]) * wet_inner


def thomas(rhs_lev, below_lev, above_lev):

    def forward(carry, item):
        ratio_prev, value_prev = carry
        rhs_here, below_here, above_here = item
        divisor = 1.0 + above_here * (1.0 - ratio_prev) + below_here
        ratio = below_here / divisor
        value = (rhs_here + above_here * value_prev) / divisor
        return ((ratio, value), (ratio, value))

    zero_level = jnp.zeros_like(rhs_lev[0])
    ratio_start = jnp.zeros_like(below_lev[0] * rhs_lev[0])
    _, (ratios, values) = lax.scan(
        forward, (ratio_start, zero_level), (rhs_lev, below_lev, above_lev), unroll=8
    )

    def backward(later, item):
        ratio, value = item
        result = value + ratio * later
        return (result, result)

    _, solved = lax.scan(backward, zero_level, (ratios, values), reverse=True, unroll=8)
    return solved


def tridiagonal(forced, coupling):
    below = jnp.repeat(coupling, 2, axis=0)
    above = jnp.concatenate([jnp.zeros_like(below[:, :1]), below[:, :-1]], axis=1)
    solved = thomas(
        jnp.moveaxis(forced, 1, 0), jnp.moveaxis(below, 1, 0), jnp.moveaxis(above, 1, 0)
    )
    return jnp.moveaxis(solved, 0, 1)


def add_totals(earlier, later):
    return earlier + later


def per_device(state, mixing, depth_levels, wind):
    fields, lev_count, col_x, col_y = state.shape
    total_x, total_y = depth_levels.shape
    start_x = lax.axis_index("gx") * col_x
    start_y = lax.axis_index("gy") * col_y
    start_z = lax.axis_index("gz") * lev_count
    padded = padded_2(state, (("gx", 2), ("gy", 3)), 1)
    row_index = (start_x - 1 + jnp.arange(col_x + 2, dtype=jnp.int32)) % total_x
    col_index = (start_y - 1 + jnp.arange(col_y + 2, dtype=jnp.int32)) % total_y
    depth_pad = jnp.take(jnp.take(depth_levels, row_index, axis=0), col_index, axis=1)
    levels = start_z + jnp.arange(lev_count, dtype=jnp.int32)
    wet_pad = (levels[:, None, None] < depth_pad[None]).astype(jnp.float32)
    density_field = density_of(padded, wet_pad)
    inclusive = jnp.cumsum(density_field, axis=0)
    column_total = inclusive[-1]
    shallower = carried_in(column_total, "gz", add_totals, jnp.zeros_like(column_total))
    pressure = 0.03 * (shallower[None] + inclusive - 0.5 * density_field)
    face_row = start_y - 1 + jnp.arange(col_y + 1, dtype=jnp.int32)
    wall_face = ((face_row >= 0) & (face_row <= total_y - 2)).astype(jnp.float32)
    row_global = start_y + jnp.arange(col_y, dtype=jnp.int32)
    coriolis = 0.5 + (row_global.astype(jnp.float32) + 0.5) / total_y
    forced = advance(padded, wet_pad, pressure, wall_face, coriolis)
    wet_inner = wet_pad[:, 1:-1, 1:-1]
    depth_inner = depth_pad[1:-1, 1:-1]
    wet_next = ((levels + 1)[:, None, None] < depth_inner[None]).astype(jnp.float32)
    top_level = (levels == 0).astype(jnp.float32)
    forced = forced.at[2:].add(wind[:, None] * top_level[None, :, None, None] * wet_inner[None])
    coupling = mixing * (wet_inner * wet_next)[None]
    whole_forced, whole_coupling = (
        lax.all_gather(forced, "gz", axis=1, tiled=True),
        lax.all_gather(coupling, "gz", axis=1, tiled=True),
    )
    solved = tridiagonal(whole_forced, whole_coupling)
    result = lax.dynamic_slice_in_dim(solved, start_z, lev_count, 1)
    return result


def solution(mesh):
    return jax.shard_map(
        per_device,
        mesh=mesh,
        in_specs=(P(None, "gz", "gx", "gy"), P(None, "gz", "gx", "gy"), P(), P(None, "gx", "gy")),
        out_specs=P(None, "gz", "gx", "gy"),
        check_vma=False,
    )
```

profile of v0, /device:TPU:1, one launch (start us, length us, event | category | flops | bytes accessed | tf_op | source)
XLA Modules:
  0.0 404.7 jit_solution(3733420670964093776)
XLA Ops:
  13.1 2.9 broadcast_multiply_fusion
  16.9 2.6 collective-permute-start
  20.1 1.9 constant_dynamic-update-slice_fusion
  24.2 2.6 fusion.103
  26.8 2.4 copy.21
  29.2 2.4 collective-permute-start.2
  31.6 2.5 copy.23
  34.1 3.0 collective-permute-start.3
  37.1 2.8 dynamic-update-slice.28
  39.9 2.8 broadcast_maximum_fusion.1
  45.2 2.9 multiply_subtract_fusion.1
  48.1 2.1 copy.22
  50.3 2.9 copy.24
  53.1 3.1 compare_select_fusion
  56.3 5.1 %fusion.106 = f32[24,34,258]{2,1,0:T(8,128)S(1)} fusion(f32[24,34,258]{2,1,0:T(8,128)S(1)} %compare_select_fusion), kind=kOutput, calls=%fused_computation.238 | output fusion | flops 4842144 | bytes 1684224 | tf_op jit(solution)/shard_map/jit(cumsum)/reduce_window_sum | solution.py:120
  63.5 2.9 multiply_subtract_fusion
  66.4 3.1 fusion.43
  70.3 13.5 %all_gather.10 = f32[4,34,258]{2,1,0:T(8,128)S(1)} all-gather(f32[1,34,258]{2,1,0:T(8,128)S(1)} %slice-done.1), channel_id=1, replica_groups=mesh['gx'=4,'gy'=8,'gz'=4] {'gz'}, dimensions={0}, use_global_device_ids=true | all-gather | bytes 175440 | tf_op jit(solution)/shard_map/all_gather | solution.py:22
  83.9 2.2 subtract_multiply_fusion
  86.3 2.6 fusion.69
  91.9 3.9 copy.20
  95.8 7.3 %broadcast_in_dim.186 = f32[2,2,96,32,256]{4,3,1,0,2:T(8,128)} broadcast(f32[2,96,32,256]{3,2,0,1:T(8,128)S(1)} %copy.20), dimensions={0,2,3,4} | broadcast | bytes 18874368 | tf_op jit(solution)/shard_map/broadcast_in_dim | solution.py:95
  103.2 13.2 %slice.499 = f32[4,95,32,256]{3,2,0,1:T(8,128)} slice(f32[4,96,32,256]{3,2,0,1:T(8,128)} %bitcast.484), slice={[0:4], [0:95], [0:32], [0:256]} | slice | bytes 24903680 | tf_op jit(solution)/shard_map/slice | solution.py:96
  116.3 12.0 %concatenate.42 = f32[4,96,32,256]{3,2,0,1:T(8,128)} pad(f32[4,95,32,256]{3,2,0,1:T(8,128)} %slice.499, f32[]{:T(128)} %constant.186.clone.1), padding=0_0x1_0x0_0x0_0 | pad | bytes 25034756 | tf_op jit(solution)/shard_map/concatenate | solution.py:96
  128.3 82.5 %all-gather.5.cloned.1.call-done = f32[4,96,32,256]{3,2,1,0:T(8,128)} async-done(((f32[4,24,32,256]{3,2,1,0:T(8,128)}), f32[4,96,32,256]{3,2,1,0:T(8,128)}) %all-gather.5.cloned.1.call-update) | async-done | bytes 12582928 | tf_op jit(solution)/shard_map/all_gather | solution.py:136
  210.8 141.2 %while.46 = (s32[]{:T(128)}, f32[4,32,256]{2,1,0:T(8,128)S(1)}, f32[4,32,256]{2,1,0:T(8,128)S(1)}, f32[12,8,4,32,256]{4,3,2,1,0:T(8,128)}, f32[12,8,4,32,256]{4,...) while((s32[]{:T(128)}, f32[4,32,256]{2,1,0:T(8,128)S(1)}, ...), condition=%wide.region_4.5_spmd.clone, body=%wide.region_3.4_spmd.clone.sunk | while | flops 2162696 | bytes 14943063 | solution.py:81
  352.0 6.2 %broadcast.313.clone = f32[12,8,4,32,256]{4,3,1,0,2:T(8,128)} broadcast(f32[]{:T(128)} %constant.186.clone.1), dimensions={} | broadcast | bytes 12582916 | tf_op jit(solution)/shard_map/broadcast.15
  358.1 35.6 %while.47 = (s32[]{:T(128)}, f32[4,32,256]{2,1,0:T(8,128)S(1)}, f32[12,8,4,32,256]{4,3,1,0,2:T(8,128)}, f32[12,8,4,32,256]{4,3,2,1,0:T(8,128)}, f32[12,8,4,32,25...) while((s32[]{:T(128)}, f32[4,32,256]{2,1,0:T(8,128)S(1)}, ...), condition=%wide.region_6.7_spmd.clone, body=%wide.region_5.6_spmd.clone.sunk | while | flops 557066 | bytes 7340315 | solution.py:90
  358.1 1.8 bitcast_dynamic-update-slice_fusion.54
  361.1 1.8 bitcast_dynamic-update-slice_fusion.54
  364.1 1.8 bitcast_dynamic-update-slice_fusion.54
  393.8 4.1 %dynamic-slice_bitcast_fusion.40 = f32[4,24,32,256]{3,2,1,0:T(8,128)} fusion(f32[96,4,32,256]{3,2,0,1:T(8,128)} %bitcast.487, s32[]{:T(128)S(6)} %select_n.96), kind=kLoop, calls=%fused_computation.139 | loop fusion | bytes 6291460 | tf_op jit(solution)/shard_map/dynamic_slice | solution.py:140
  (318 shorter events, 188.9 us)
Async XLA Ops:
  6.5 1.2 copy-start
  6.5 85.4 %all-gather.3.cloned.1.call-start = ((), (), s32[]{:S(2)}) async-start(), calls=%async_computation | async-start | bytes 7864320 | tf_op jit(solution)/shard_map/all_gather | solution.py:137
  10.3 0.5 copy-start.18
  10.8 1.1 copy-start.5
  13.1 3.0 copy-start.2
  16.1 194.8 %all-gather.5.cloned.1.call-start = ((), (), s32[]{:S(2)}) async-start(), calls=%async_computation.1 | async-start | bytes 15728640 | tf_op jit(solution)/shard_map/all_gather | solution.py:136
  16.9 5.6 %collective-permute-start = (f32[4,24,1,256]{3,2,1,0:T(1,128)}, f32[4,24,1,256]{3,2,1,0:T(1,128)S(1)}, u32[]{:S(2)}, u32[]{:S(2)}) collective-permute-start(f32[4,24,1,256]{3,2,1,0:T(1,128)} %get-tuple-element.347), channel_id=1, source_target_pairs={{0,32},{32,64},{64,96},{96,0},{1,33},{33,65},{65,97},{97,1},{2,34}... | collective-permute-start | bytes 294920 | tf_op jit(solution)/shard_map/ppermute | solution.py:14
  19.5 4.0 collective-permute-start.1
  29.2 19.0 %collective-permute-start.2 = (f32[4,24,34,1]{2,1,3,0:T(8,128)S(1)}, f32[4,24,34,1]{2,1,3,0:T(8,128)S(1)}, u32[]{:S(2)}, u32[]{:S(2)}) collective-permute-start(f32[4,24,34,1]{2,1,3,0:T(8,128)S(1)} %copy.21), channel_id=1, source_target_pairs={{0,4},{4,8},{8,12},{12,16},{16,20},{20,24},{24,28},{28,0},{1,5},{5... | collective-permute-start | bytes 39176 | tf_op jit(solution)/shard_map/ppermute | solution.py:14
  34.1 16.2 %collective-permute-start.3 = (f32[4,24,34,1]{2,1,3,0:T(8,128)S(1)}, f32[4,24,34,1]{2,1,3,0:T(8,128)}, u32[]{:S(2)}, u32[]{:S(2)}) collective-permute-start(f32[4,24,34,1]{2,1,3,0:T(8,128)S(1)} %copy.23), channel_id=1, source_target_pairs={{4,0},{8,4},{12,8},{16,12},{20,16},{24,20},{28,24},{0,28},{5,1},{9... | collective-permute-start | bytes 39176 | tf_op jit(solution)/shard_map/ppermute | solution.py:15
  42.7 1.0 copy-start.13
  42.7 2.5 copy-start.9
  48.1 5.0 %copy-start.19 = (s32[24]{0:T(128)S(1)}, s32[24]{0:T(128)}, u32[]{:S(2)}) copy-start(s32[24]{0:T(128)} %copy-done.18) | copy-start | bytes 292
  53.1 8.2 %copy-start.4 = (f32[4,24,34,1]{3,2,1,0:T(8,128)S(1)}, f32[4,24,34,1]{3,2,1,0:T(8,128)}, u32[]{:S(2)}) copy-start(f32[4,24,34,1]{3,2,1,0:T(8,128)} %copy.24) | copy-start | bytes 39172
  53.1 8.2 %copy-start.6 = (f32[24,34,258]{2,1,0:T(8,128)S(1)}, f32[24,34,258]{2,1,0:T(8,128)}, u32[]{:S(2)}) copy-start(f32[24,34,258]{2,1,0:T(8,128)} %copy-done.5) | copy-start | bytes 2526340
  56.3 6.1 %copy-start.10 = (f32[24,34,258]{2,1,0:T(8,128)}, f32[24,34,258]{2,1,0:T(8,128)S(1)}, u32[]{:S(2)}) copy-start(f32[24,34,258]{2,1,0:T(8,128)S(1)} %compare_select_fusion) | copy-start | bytes 2526340
  56.3 5.1 %copy-start.3 = (f32[4,24,34,1]{3,2,1,0:T(8,128)S(1)}, f32[4,24,34,1]{3,2,1,0:T(8,128)}, u32[]{:S(2)}) copy-start(f32[4,24,34,1]{3,2,1,0:T(8,128)} %copy.22) | copy-start | bytes 39172
  61.3 1.1 copy-start.16
  62.5 1.0 copy-start.11
  63.5 2.9 copy-start.7
  69.5 0.8 slice-start.1
  70.3 15.7 %copy-start.20 = (f32[256]{0:T(256)S(1)}, f32[256]{0:T(256)}, u32[]{:S(2)}) copy-start(f32[256]{0:T(256)} %add_multiply_fusion) | copy-start | bytes 3076
  83.9 2.2 copy-start.12
  83.9 2.4 copy-start.14
  86.3 2.6 slice-start
  86.3 2.6 copy-start.15
  89.0 0.8 copy-start.17
  89.0 0.8 copy-start.21
  90.2 1.7 copy-start.8
  393.8 4.1 %copy-start.1 = (s32[128,2048]{1,0:T(8,128)S(1)}, s32[128,2048]{1,0:T(8,128)}, u32[]{:S(2)}) copy-start(s32[128,2048]{1,0:T(8,128)} %param.14) | copy-start | bytes 3145732
Sparse Core Ops, SparseCore 0:
  16.2 70.8 all-gather.2
  92.0 118.8 all-gather.4
where the time goes:
time: 408 us; the launch traced here: 405 us
  other arithmetic  177 us (43%)
  local copies, waits for them, and re-layouts  107 us (26%)
  waiting for transfers between devices  83.6 us (20%)
  between operations  13.8 us (3%)
  blocking collectives  13.5 us (3%)
  starting transfers between devices  8.1 us (2%)
    while x96, other arithmetic  118 us
    all_gather x1, waiting for transfers between devices, per_device(): lax.all_gather(forced, 'gz', axis=1, tiled=True)  82.5 us
    dynamic_update_slice x24, local copies, waits for them, and re-layouts, thomas(): lax.scan(forward, (ratio_start, zero_level), (rhs_lev, below_lev, above_l...  30.6 us
    concatenate x24, other arithmetic, thomas(): lax.scan(forward, (ratio_start, zero_level), (rhs_lev, below_lev, above_l...  25.3 us
    all_gather x1, blocking collectives, carried_in(): gathered = lax.all_gather(part, axis)  13.5 us
    slice x1, local copies, waits for them, and re-layouts, tridiagonal(): below[:, :-1]  13.2 us
    concatenate x1, local copies, waits for them, and re-layouts, tridiagonal(): jnp.concatenate([jnp.zeros_like(below[:, :1]), below[:, :-1]], axis=1)  12 us
    unnamed x45, local copies, waits for them, and re-layouts  9.96 us
  transfers between devices with their start and end apart: 6, of which 2 were waited for; matrix products, arithmetic and copies ran while one was open for 20% of the time, Pallas kernels for 0%

commit v1 on v0

--- a/solution.py
+++ b/solution.py
@@ -1,7 +1,19 @@
+import functools
 import jax
 import jax.numpy as jnp
 from jax import lax
 from jax.sharding import PartitionSpec as P
+
+
+def bind_wall(sheet, axis_no):
+    r_now = jnp.concatenate(
+        lax.all_to_all(jnp.stack([sheet] * lax.axis_size("gz")), "gz", concat_axis=0, split_axis=0),
+        axis_no,
+    )
+    return r_now
+
+
+bring_page_up = functools.partial(bind_wall, axis_no=1)
 
 
 def padded_2(array, sides, width):
@@ -133,7 +145,7 @@
     forced = forced.at[2:].add(wind[:, None] * top_level[None, :, None, None] * wet_inner[None])
     coupling = mixing * (wet_inner * wet_next)[None]
     whole_forced, whole_coupling = (
-        lax.all_gather(forced, "gz", axis=1, tiled=True),
+        bring_page_up(forced),
         lax.all_gather(coupling, "gz", axis=1, tiled=True),
     )
     solved = tridiagonal(whole_forced, whole_coupling)

time: 408 us -> 447 us (1.096)
  waiting for transfers between devices: 83.6 us -> 102 us
  other arithmetic: 177 us -> 184 us
  starting transfers between devices: 8.1 us -> 14.5 us
  local copies, waits for them, and re-layouts: 107 us -> 112 us
    all_to_all x0 -> x1, waiting for transfers between devices: none -> 102 us  [bind_wall(): lax.all_to_all(jnp.stack([sheet] * lax.axis_size('gz')), 'gz', concat_axi...]
    all_gather x1 -> x0, waiting for transfers between devices: 82.5 us -> none  [per_device(): lax.all_gather(forced, 'gz', axis=1, tiled=True)]
    all_to_all x0 -> x1, starting transfers between devices: none -> 6.52 us  [bind_wall(): lax.all_to_all(jnp.stack([sheet] * lax.axis_size('gz')), 'gz', concat_axi...]
    another operation x1 -> x2, local copies, waits for them, and re-layouts: 6.16 us -> 12.2 us
    unnamed x45 -> x29, local copies, waits for them, and re-layouts: 9.96 us -> 12.2 us
  transfers between devices with their start and end apart: 6 -> 6, of which waited for: 2 -> 1; matrix products, arithmetic and copies ran while one was open for 20% -> 23% of each run, Pallas kernels for 0% -> 0%
where the time goes in v1:
time: 447 us; the launch traced here: 441 us
  other arithmetic  184 us (41%)
  local copies, waits for them, and re-layouts  112 us (25%)
  waiting for transfers between devices  102 us (23%)
  starting transfers between devices  14.5 us (3%)
  between operations  13.8 us (3%)
  blocking collectives  13.4 us (3%)
    while x96, other arithmetic  118 us
    all_to_all x1, waiting for transfers between devices, bind_wall(): lax.all_to_all(jnp.stack([sheet] * lax.axis_size('gz')), 'gz', concat_axi...  102 us
    dynamic_update_slice x24, local copies, waits for them, and re-layouts, thomas(): lax.scan(forward, (ratio_start, zero_level), (rhs_lev, below_lev, above_l...  31.5 us
    concatenate x24, other arithmetic, thomas(): lax.scan(forward, (ratio_start, zero_level), (rhs_lev, below_lev, above_l...  25.3 us
    all_gather x1, blocking collectives, carried_in(): gathered = lax.all_gather(part, axis)  13.4 us
    unnamed x29, local copies, waits for them, and re-layouts  12.2 us
    concatenate x1, local copies, waits for them, and re-layouts, tridiagonal(): jnp.concatenate([jnp.zeros_like(below[:, :1]), below[:, :-1]], axis=1)  11.8 us
    slice x1, local copies, waits for them, and re-layouts, tridiagonal(): below[:, :-1]  11.7 us
  transfers between devices with their start and end apart: 6, of which 1 were waited for; matrix products, arithmetic and copies ran while one was open for 23% of the time, Pallas kernels for 0%

profile of v1, /device:TPU:1, one launch (start us, length us, event | category | flops | bytes accessed | tf_op | source)
XLA Modules:
  0.0 441.1 jit_solution(5483393616034429387)
XLA Ops:
  8.1 2.7 collective-permute-start
  15.1 2.8 broadcast_multiply_fusion
  18.0 4.0 constant_dynamic-update-slice_fusion
  22.0 2.5 pad_maximum_fusion.7
  24.5 2.6 fusion.103
  27.1 2.3 copy.21
  29.4 2.5 collective-permute-start.2
  31.9 2.4 copy.23
  34.3 2.8 collective-permute-start.3
  37.1 2.8 dynamic-update-slice.30
  39.9 2.2 broadcast_maximum_fusion.1
  44.1 2.9 multiply_subtract_fusion.1
  47.8 2.1 copy.24
  49.9 3.2 compare_select_fusion
  54.2 5.0 %fusion.106 = f32[24,34,258]{2,1,0:T(8,128)S(1)} fusion(f32[24,34,258]{2,1,0:T(8,128)S(1)} %compare_select_fusion), kind=kOutput, calls=%fused_computation.238 | output fusion | flops 4842144 | bytes 1684224 | tf_op jit(solution)/shard_map/jit(cumsum)/reduce_window_sum | solution.py:132
  60.3 13.4 %all_gather.7 = f32[4,34,258]{2,1,0:T(8,128)S(1)} all-gather(f32[1,34,258]{2,1,0:T(8,128)S(1)} %slice.516), channel_id=1, replica_groups=mesh['gx'=4,'gy'=8,'gz'=4] {'gz'}, dimensions={0}, use_global_device_ids=true | all-gather | bytes 175440 | tf_op jit(solution)/shard_map/all_gather | solution.py:34
  73.8 2.2 subtract_multiply_fusion
  76.2 3.2 broadcast_maximum_fusion
  81.7 4.2 multiply_subtract_fusion
  85.9 6.6 %fusion.43 = f32[4,24,32,256]{3,2,1,0:T(8,128)} fusion(f32[4,24,32,256]{3,2,1,0:T(8,128)S(1)} %copy-done.3, f32[4,24,32,257]{3,2,1,0:T(8,128)} %multiply_subtract_fusion, f32[4,24,33,256]{3,2,1,0:T(8,128)S(1)} %copy-done.6), kind=kLoop, calls=%fused_computation.135 | loop fusion | flops 3145728 | bytes 18874368 | tf_op jit(solution)/shard_map/sub | solution.py:63
  93.8 2.6 fusion.69
  98.0 6.1 %stack.20 = f32[4,4,24,32,256]{4,3,1,2,0:T(8,128)} broadcast(f32[4,24,32,256]{3,2,0,1:T(8,128)S(1)} %copy.27), dimensions={1,2,3,4} | broadcast | bytes 15728640 | tf_op jit(solution)/shard_map/stack | solution.py:10
  104.1 6.5 %all-to-all-start = ((f32[4,4,24,32,256]{4,3,1,2,0:T(8,128)}), f32[4,4,24,32,256]{4,3,1,2,0:T(8,128)}, u32[]{:S(2)}, u32[]{:S(2)}) async-start(f32[4,4,24,32,256]{4,3,1,2,0:T(8,128)} %stack.20), calls=%async_computation | async-start | bytes 25165824 | tf_op jit(solution)/shard_map/all_to_all | solution.py:10
  110.7 3.9 copy.20
  114.6 6.7 %broadcast_in_dim.186 = f32[2,2,96,32,256]{4,3,1,0,2:T(8,128)} broadcast(f32[2,96,32,256]{3,2,0,1:T(8,128)S(1)} %copy.20), dimensions={0,2,3,4} | broadcast | bytes 18874368 | tf_op jit(solution)/shard_map/broadcast_in_dim | solution.py:107
  121.3 11.7 %slice.499 = f32[4,95,32,256]{3,2,0,1:T(8,128)} slice(f32[4,96,32,256]{3,2,0,1:T(8,128)} %bitcast.472), slice={[0:4], [0:95], [0:32], [0:256]} | slice | bytes 24903680 | tf_op jit(solution)/shard_map/slice | solution.py:108
  133.1 11.8 %concatenate.46 = f32[4,96,32,256]{3,2,0,1:T(8,128)} pad(f32[4,95,32,256]{3,2,0,1:T(8,128)} %slice.499, f32[]{:T(128)} %constant.188.clone.1), padding=0_0x1_0x0_0x0_0 | pad | bytes 25034756 | tf_op jit(solution)/shard_map/concatenate | solution.py:108
  144.9 101.6 %all-to-all-done = f32[4,4,24,32,256]{4,3,1,2,0:T(8,128)} async-done(((f32[4,4,24,32,256]{4,3,1,2,0:T(8,128)}), f32[4,4,24,32,256]{4,3,1,2,0:T(8,128)}, u32[]{:S(2)}, u32[]{:S(2)}) %all-to-all-start) | async-done | bytes 12582944 | tf_op jit(solution)/shard_map/all_to_all | solution.py:10
  246.5 141.6 %while.46 = (s32[]{:T(128)}, f32[4,32,256]{2,1,0:T(8,128)S(1)}, f32[4,32,256]{2,1,0:T(8,128)S(1)}, f32[12,8,4,32,256]{4,3,2,1,0:T(8,128)}, f32[12,8,4,32,256]{4,...) while((s32[]{:T(128)}, f32[4,32,256]{2,1,0:T(8,128)S(1)}, ...), condition=%wide.region_4.5_spmd.clone, body=%wide.region_3.4_spmd.clone.sunk | while | flops 2162696 | bytes 14943063 | solution.py:93
  388.1 6.1 %broadcast.318.clone = f32[12,8,4,32,256]{4,3,1,0,2:T(8,128)} broadcast(f32[]{:T(128)} %constant.188.clone.1), dimensions={} | broadcast | bytes 12582916 | tf_op jit(solution)/shard_map/broadcast.15
  394.2 36.0 %while.47 = (s32[]{:T(128)}, f32[4,32,256]{2,1,0:T(8,128)S(1)}, f32[12,8,4,32,256]{4,3,1,0,2:T(8,128)}, f32[12,8,4,32,256]{4,3,2,1,0:T(8,128)}, f32[12,8,4,32,25...) while((s32[]{:T(128)}, f32[4,32,256]{2,1,0:T(8,128)S(1)}, ...), condition=%wide.region_6.7_spmd.clone, body=%wide.region_5.6_spmd.clone.sunk | while | flops 557066 | bytes 7340315 | solution.py:102
  430.2 4.1 dynamic-slice_bitcast_fusion.40
  (302 shorter events, 192.6 us)
Async XLA Ops:
  6.5 4.4 copy-start
  6.5 104.2 %all-gather.2.cloned.1.call-start = ((), (), s32[]{:S(2)}) async-start(), calls=%async_computation.1 | async-start | bytes 7864320 | tf_op jit(solution)/shard_map/all_gather | solution.py:149
  8.1 13.9 %collective-permute-start = (f32[4,24,1,256]{3,2,1,0:T(1,128)S(1)}, f32[4,24,1,256]{3,2,1,0:T(1,128)S(1)}, u32[]{:S(2)}, u32[]{:S(2)}) collective-permute-start(f32[4,24,1,256]{3,2,1,0:T(1,128)S(1)} %get-tuple-element.323), channel_id=1, source_target_pairs={{0,32},{32,64},{64,96},{96,0},{1,33},{33,65},{65,97},{97,1},{2,34}... | collective-permute-start | bytes 294920 | tf_op jit(solution)/shard_map/ppermute | solution.py:26
  10.8 11.2 %collective-permute-start.1 = (f32[4,24,1,256]{3,2,1,0:T(1,128)S(1)}, f32[4,24,1,256]{3,2,1,0:T(1,128)S(1)}, u32[]{:S(2)}, u32[]{:S(2)}) collective-permute-start(f32[4,24,1,256]{3,2,1,0:T(1,128)S(1)} %get-tuple-element.324), channel_id=1, source_target_pairs={{32,0},{64,32},{96,64},{0,96},{33,1},{65,33},{97,65},{1,97},{34,2}... | collective-permute-start | bytes 294920 | tf_op jit(solution)/shard_map/ppermute | solution.py:27
  13.7 26.2 %copy-start.5 = (f32[24,34,258]{2,1,0:T(8,128)}, f32[24,34,258]{2,1,0:T(8,128)S(1)}, u32[]{:S(2)}) copy-start(f32[24,34,258]{2,1,0:T(8,128)S(1)} %compare_convert_fusion) | copy-start | bytes 2526340
  29.4 17.6 %collective-permute-start.2 = (f32[4,24,34,1]{2,1,3,0:T(8,128)S(1)}, f32[4,24,34,1]{2,1,3,0:T(8,128)S(1)}, u32[]{:S(2)}, u32[]{:S(2)}) collective-permute-start(f32[4,24,34,1]{2,1,3,0:T(8,128)S(1)} %copy.21), channel_id=1, source_target_pairs={{0,4},{4,8},{8,12},{12,16},{16,20},{20,24},{24,28},{28,0},{1,5},{5... | collective-permute-start | bytes 39176 | tf_op jit(solution)/shard_map/ppermute | solution.py:26
  34.3 13.5 %collective-permute-start.3 = (f32[4,24,34,1]{2,1,3,0:T(8,128)S(1)}, f32[4,24,34,1]{2,1,3,0:T(8,128)S(1)}, u32[]{:S(2)}, u32[]{:S(2)}) collective-permute-start(f32[4,24,34,1]{2,1,3,0:T(8,128)S(1)} %copy.23), channel_id=1, source_target_pairs={{4,0},{8,4},{12,8},{16,12},{20,16},{24,20},{28,24},{0,28},{5,1},{9... | collective-permute-start | bytes 39176 | tf_op jit(solution)/shard_map/ppermute | solution.py:27
  39.9 2.8 copy-start.7
  42.1 2.0 copy-start.2
  53.1 1.1 copy-start.8
  59.1 1.1 copy-start.12
  73.8 2.4 copy-start.4
  79.4 1.0 copy-start.9
  79.4 2.3 copy-start.3
  81.7 4.2 copy-start.6
  92.5 1.3 copy-start.10
  93.8 2.6 slice-start
  93.8 2.6 copy-start.11
  96.4 0.8 copy-start.13
  104.1 142.4 %all-to-all-start = ((f32[4,4,24,32,256]{4,3,1,2,0:T(8,128)}), f32[4,4,24,32,256]{4,3,1,2,0:T(8,128)}, u32[]{:S(2)}, u32[]{:S(2)}) async-start(f32[4,4,24,32,256]{4,3,1,2,0:T(8,128)} %stack.20), calls=%async_computation | async-start | bytes 25165824 | tf_op jit(solution)/shard_map/all_to_all | solution.py:10
  430.2 4.1 copy-start.1
Sparse Core Ops, SparseCore 0:
  18.1 70.0 all-gather.1
